TPU v7x, 1024 devices: a whole 8x8x8 slice. The times are simulated.
1024 devices in a mesh: batch: 8 (over z), seq: 8 (over x), head: 16 (over y, core).
Axes of the slice: x: 8, y: 8, z: 8, core: 2. Of those that a mesh axis runs over, the one named last changes fastest.
Arguments:
- queries: bfloat16 [40960, 8192], P(('batch', 'seq', 'head')), parts along dimension 0, may hold values from -6 to 6
- keys: bfloat16 [40960, 8192], P(('batch', 'seq', 'head')), parts along dimension 0, may hold values from -6 to 6
- values: bfloat16 [40960, 8192], P(('batch', 'seq', 'head')), parts along dimension 0, may hold values from -6 to 6
- group_order: int32 [64, 2], P(('batch', 'seq')), parts along dimension 0, may hold values from 0 to 15, as said below
- gain: float32 [8192], P('head'), may hold values from 0.1 to 1.9
Outputs:
- attended: bfloat16 [40960, 8192], P(('batch', 'seq'), 'head'), parts along dimension 0
There are 8 independent parts, one for each index of `batch`. A program takes and returns all parts, laid end to end along the dimension named above; an argument that names none is the same for every part. Nothing has to cross between parts.
Inputs may be any that keep to these rules, and one draw needn't show every extreme that they name: `group_order`: row d holds d and 15 - d, in either order.
All inputs are finite; a program needn't handle non-finite values.
Results may differ from a plain program's by a relative error of at most 0.01.
Values may be sent and summed in bfloat16 or wider, within the bound.
No kernel may reach another device: no remote copies, remote signals or barrier semaphores. Data moves between devices by JAX's collectives and lax.ppermute only.
A program may use at most 32 MiB of HBM per device.

v0:
```python
import jax
import jax.numpy as jnp
from jax import lax
from jax.sharding import PartitionSpec as P

DH = 128


def local(queries, keys, values, group_order, gain):
    q_all, k_all, v_all = (
        lax.all_to_all(queries, "head", split_axis=1, concat_axis=0, tiled=True),
        lax.all_to_all(keys, "head", split_axis=1, concat_axis=0, tiled=True),
        lax.all_to_all(values, "head", split_axis=1, concat_axis=0, tiled=True),
    )
    rows = q_all.shape[0]
    half = rows // 2
    local_heads = gain.shape[0] // DH
    pairs = lax.axis_size("seq")
    here = lax.axis_index("seq")
    qx = q_all.reshape(rows, local_heads, DH)
    kx = k_all.reshape(rows, local_heads, DH)
    vx = v_all.reshape(rows, local_heads, DH)
    kh = kx.reshape(2, half, local_heads, DH)
    vh = vx.reshape(2, half, local_heads, DH)
    state = jnp.einsum("jthd,jthe->jhde", kh, vh, preferred_element_type=jnp.float32).astype(
        jnp.bfloat16
    )
    state = lax.optimization_barrier(state).astype(jnp.float32)
    order = group_order[0]
    low_first = order[0] < pairs
    lows = jnp.where(low_first, state[0], state[1])
    highs = jnp.where(low_first, state[1], state[0])
    empty = jnp.zeros_like(lows)
    low_sum = empty
    high_sum = empty
    piece_low = lax.all_gather(lows[None].astype(jnp.bfloat16), "seq", axis=0, tiled=True).astype(
        jnp.float32
    )
    piece_high = lax.all_gather(highs[None].astype(jnp.bfloat16), "seq", axis=0, tiled=True).astype(
        jnp.float32
    )
    owners = jnp.arange(piece_low.shape[0], dtype=jnp.int32)
    below = (owners < here).astype(jnp.float32)[:, None, None, None]
    other = (owners != here).astype(jnp.float32)[:, None, None, None]
    above = (owners > here).astype(jnp.float32)[:, None, None, None]
    low_sum = low_sum + jnp.sum(piece_low * below, axis=0)
    high_sum = high_sum + jnp.sum(piece_low * other + piece_high * above, axis=0)
    first_pre = jnp.where(low_first, low_sum, high_sum).astype(jnp.bfloat16)
    second_pre = jnp.where(low_first, high_sum, low_sum).astype(jnp.bfloat16)
    index = jnp.arange(rows, dtype=jnp.int32)
    position = order[index // half] * half + index % half
    scores = jnp.einsum("thd,shd->hts", qx, kx, preferred_element_type=jnp.float32)
    allowed = position[:, None] >= position[None, :]
    scores = jnp.where(allowed[None], scores, 0.0).astype(jnp.bfloat16)
    intra = jnp.einsum("hts,she->the", scores, vx, preferred_element_type=jnp.float32)
    qh = qx.reshape(2, half, local_heads, DH)
    first_term = jnp.einsum("thd,hde->the", qh[0], first_pre, preferred_element_type=jnp.float32)
    second_term = jnp.einsum("thd,hde->the", qh[1], second_pre, preferred_element_type=jnp.float32)
    raw = intra + jnp.concatenate([first_term, second_term], axis=0)
    scale = lax.rsqrt(jnp.mean(raw * raw, axis=-1, keepdims=True) + 1e-06)
    gains = gain.reshape(local_heads, DH)
    return (raw * scale * gains).astype(jnp.bfloat16).reshape(rows, local_heads * DH)


def solution(mesh):
    return jax.shard_map(
        local,
        mesh=mesh,
        in_specs=(
            P(("batch", "seq", "head"), None),
            P(("batch", "seq", "head"), None),
            P(("batch", "seq", "head"), None),
            P(("batch", "seq"), None),
            P("head"),
        ),
        out_specs=P(("batch", "seq"), "head"),
        check_vma=False,
    )
```

profile of v0, /device:TPU:2, one launch (start us, length us, event | category | flops | bytes accessed | tf_op | source)
XLA Modules:
  0.0 171.0 jit_solution(2252467731232683023)
XLA Ops:
  6.5 2.0 %copy.65 = bf16[5,16,8,512]{3,2,0,1:T(8,128)(2,1)} copy(bf16[5,16,8,512]{3,2,1,0:T(8,128)(2,1)} %bitcast.35) | data formatting | bytes 1310720 | tf_op jit(solution)/shard_map/all_to_all | solution.py:12
  8.6 7.7 %all-to-all-start.1 = ((bf16[40,16,512]{2,0,1:T(8,128)(2,1)}), bf16[40,16,512]{2,0,1:T(8,128)(2,1)S(1)}, u32[]{:S(2)}, u32[]{:S(2)}) async-start(bf16[40,16,512]{2,0,1:T(8,128)(2,1)} %bitcast.26), calls=%async_computation.1 | async-start | bytes 1310720 | tf_op jit(solution)/shard_map/all_to_all | solution.py:12
  16.3 0.9 copy.64
  17.1 17.4 %all-to-all-done.1 = bf16[40,16,512]{2,0,1:T(8,128)(2,1)S(1)} async-done(((bf16[40,16,512]{2,0,1:T(8,128)(2,1)}), bf16[40,16,512]{2,0,1:T(8,128)(2,1)S(1)}, u32[]{:S(2)}, u32[]{:S(2)}) %all-to-all-start.1) | async-done | bytes 655392 | tf_op jit(solution)/shard_map/all_to_all | solution.py:12
  34.5 4.7 %all-to-all-start.2 = ((bf16[40,16,512]{2,0,1:T(8,128)(2,1)}), bf16[40,16,512]{2,0,1:T(8,128)(2,1)S(1)}, u32[]{:S(2)}, u32[]{:S(2)}) async-start(bf16[40,16,512]{2,0,1:T(8,128)(2,1)} %bitcast.25), calls=%async_computation.2 | async-start | bytes 1310720 | tf_op jit(solution)/shard_map/all_to_all | solution.py:13
  39.2 0.0 all-gather.3.cloned.1.call-start
  39.3 0.6 fusion.29
  40.6 0.2 reshape_reshape.7
  40.8 16.8 %all-to-all-done.2 = bf16[40,16,512]{2,0,1:T(8,128)(2,1)S(1)} async-done(((bf16[40,16,512]{2,0,1:T(8,128)(2,1)}), bf16[40,16,512]{2,0,1:T(8,128)(2,1)S(1)}, u32[]{:S(2)}, u32[]{:S(2)}) %all-to-all-start.2) | async-done | bytes 655392 | tf_op jit(solution)/shard_map/all_to_all | solution.py:13
  57.6 0.2 reshape_reshape.8
  57.8 0.4 convolution_convert_fusion
  58.3 0.7 select_convert_fusion.8
  59.0 0.0 all-gather.5.cloned.1.call-start
  59.1 0.7 all-gather.5.cloned.1.call-update
  59.8 0.9 copy.66
  60.7 4.6 %all-to-all-start = ((bf16[40,16,512]{2,0,1:T(8,128)(2,1)}), bf16[40,16,512]{2,0,1:T(8,128)(2,1)S(1)}, u32[]{:S(2)}, u32[]{:S(2)}) async-start(bf16[40,16,512]{2,0,1:T(8,128)(2,1)} %bitcast.27), calls=%async_computation | async-start | bytes 1310720 | tf_op jit(solution)/shard_map/all_to_all | solution.py:11
  65.3 1.4 fusion.26
  66.7 1.1 broadcast_compare_fusion
  67.7 0.2 reshape.155
  67.9 1.0 reshape.156
  68.9 14.8 %all-to-all-done = bf16[40,16,512]{2,0,1:T(8,128)(2,1)S(1)} async-done(((bf16[40,16,512]{2,0,1:T(8,128)(2,1)}), bf16[40,16,512]{2,0,1:T(8,128)(2,1)S(1)}, u32[]{:S(2)}, u32[]{:S(2)}) %all-to-all-start) | async-done | bytes 655392 | tf_op jit(solution)/shard_map/all_to_all | solution.py:11
  83.7 1.0 reshape.154
  84.7 0.1 squeeze.7
  84.8 0.1 squeeze.16
  84.9 26.0 %all-gather.3.cloned.1.call-done = bf16[8,4,128,128]{3,2,1,0:T(8,128)(2,1)} async-done(((bf16[1,4,128,128]{3,2,1,0:T(8,128)(2,1)}), bf16[8,4,128,128]{3,2,1,0:T(8,128)(2,1)}) %all-gather.3.cloned.1.call-update) | async-done | bytes 1048592 | tf_op jit(solution)/shard_map/all_gather | solution.py:36
  110.9 45.7 %all-gather.5.cloned.1.call-done = bf16[8,4,128,128]{3,2,1,0:T(8,128)(2,1)} async-done(((bf16[1,4,128,128]{3,2,1,0:T(8,128)(2,1)}), bf16[8,4,128,128]{3,2,1,0:T(8,128)(2,1)}) %all-gather.5.cloned.1.call-update) | async-done | bytes 1048592 | tf_op jit(solution)/shard_map/all_gather | solution.py:39
  156.5 2.2 %fusion.5 = (bf16[4,128,128]{2,1,0:T(8,128)(2,1)S(1)}, bf16[4,128,128]{2,1,0:T(8,128)(2,1)S(1)}) fusion(bf16[8,4,128,128]{3,2,1,0:T(8,128)(2,1)} %all-gather.3.cloned.1.call-done, f32[8]{0:T(128)S(1)} %compare_convert_fusion.2, f32[8]{0:T(128)S(1)} %get-tuple-element.15, bf16[8,4,128,128]{3,2,1,0:T(8,128)(2,1)} %all-gather.5.cloned.1.call-done, ...), kind=kLoop, calls=%fused_computation.7 | loop fusion | flops 4063232 | bytes 2359392 | tf_op jit(solution)/shard_map/reduce_sum | solution.py:46
  158.7 0.3 convolution_bitcast_fusion.1
  159.0 0.3 convolution_bitcast_fusion
  159.4 3.4 %multiply_reduce_fusion = (f32[640,4]{0,1:T(4,128)S(1)}, f32[640,4,128]{0,2,1:T(8,128)S(1)}) fusion(f32[320,4,128]{0,2,1:T(8,128)S(1)} %convolution_bitcast_fusion, f32[320,4,128]{0,2,1:T(8,128)S(1)} %convolution_bitcast_fusion.1, bf16[640,4,128]{2,1,0:T(4,128)(2,1)} %reshape.156, pred[640,640]{1,0:T(8,128)(4,1)} %broadcast_compare_fusion, ...), kind=kOutput, calls=%fused_computation.13 | convolution fusion | flops 843445760 | bytes 5007360 | tf_op jit(solution)/shard_map/hts,she->the/dot_general | solution.py:55
  162.8 0.2 multiply_convert_fusion
  163.0 1.1 copy.33
  (14 shorter events, 0.1 us)
Async XLA Ops:
  6.5 9.7 %copy-start = (bf16[40,8192]{1,0:T(8,128)(2,1)S(1)}, bf16[40,8192]{1,0:T(8,128)(2,1)}, u32[]{:S(2)}) copy-start(bf16[40,8192]{1,0:T(8,128)(2,1)} %param.7) | copy-start | bytes 1966084
  8.6 25.9 %all-to-all-start.1 = ((bf16[40,16,512]{2,0,1:T(8,128)(2,1)}), bf16[40,16,512]{2,0,1:T(8,128)(2,1)S(1)}, u32[]{:S(2)}, u32[]{:S(2)}) async-start(bf16[40,16,512]{2,0,1:T(8,128)(2,1)} %bitcast.26), calls=%async_computation.1 | async-start | bytes 1310720 | tf_op jit(solution)/shard_map/all_to_all | solution.py:12
  16.3 23.0 %copy-start.2 = (s32[1,2]{1,0:T(1,128)S(1)}, s32[1,2]{1,0:T(1,128)}, u32[]{:S(2)}) copy-start(s32[1,2]{1,0:T(1,128)} %param.8) | copy-start | bytes 28
  34.5 23.1 %all-to-all-start.2 = ((bf16[40,16,512]{2,0,1:T(8,128)(2,1)}), bf16[40,16,512]{2,0,1:T(8,128)(2,1)S(1)}, u32[]{:S(2)}, u32[]{:S(2)}) async-start(bf16[40,16,512]{2,0,1:T(8,128)(2,1)} %bitcast.25), calls=%async_computation.2 | async-start | bytes 1310720 | tf_op jit(solution)/shard_map/all_to_all | solution.py:13
  39.2 71.6 %all-gather.3.cloned.1.call-start = ((), (), s32[]{:S(2)}) async-start(), calls=%async_computation.3 | async-start | bytes 1179648 | tf_op jit(solution)/shard_map/all_gather | solution.py:36
  57.8 2.0 %copy-start.1 = (bf16[40,8192]{1,0:T(8,128)(2,1)S(1)}, bf16[40,8192]{1,0:T(8,128)(2,1)}, u32[]{:S(2)}) copy-start(bf16[40,8192]{1,0:T(8,128)(2,1)} %param.5) | copy-start | bytes 1966084
  59.0 97.5 %all-gather.5.cloned.1.call-start = ((), (), s32[]{:S(2)}) async-start(), calls=%async_computation.4 | async-start | bytes 1179648 | tf_op jit(solution)/shard_map/all_gather | solution.py:39
  60.7 23.0 %all-to-all-start = ((bf16[40,16,512]{2,0,1:T(8,128)(2,1)}), bf16[40,16,512]{2,0,1:T(8,128)(2,1)S(1)}, u32[]{:S(2)}, u32[]{:S(2)}) async-start(bf16[40,16,512]{2,0,1:T(8,128)(2,1)} %bitcast.27), calls=%async_computation | async-start | bytes 1310720 | tf_op jit(solution)/shard_map/all_to_all | solution.py:11
  159.4 3.5 %copy-start.3 = (f32[512]{0:T(512)S(1)}, f32[512]{0:T(512)}, u32[]{:S(2)}) copy-start(f32[512]{0:T(512)} %param.9) | copy-start | bytes 6148
Sparse Core Ops, SparseCore 0:
  59.1 51.6 all-gather.2
  113.5 42.9 all-gather.4
where the time goes:
time: 171 us
  waiting for transfers between devices  121 us (71%)
  starting transfers between devices  17.1 us (10%)
  between operations  14.3 us (8%)
  local copies, waits for them, and re-layouts  8.22 us (5%)
  other arithmetic  5.54 us (3%)
  matrix products  4.52 us (3%)
    all_gather x1, waiting for transfers between devices, local(): lax.all_gather(highs[None].astype(jnp.bfloat16), 'seq', axis=0, tiled=True)  45.7 us
    all_gather x1, waiting for transfers between devices, local(): lax.all_gather(lows[None].astype(jnp.bfloat16), 'seq', axis=0, tiled=True)  26 us
    all_to_all x1, waiting for transfers between devices, local(): lax.all_to_all(keys, 'head', split_axis=1, concat_axis=0, tiled=True)  17.4 us
    all_to_all x1, waiting for transfers between devices, local(): lax.all_to_all(values, 'head', split_axis=1, concat_axis=0, tiled=True)  16.8 us
    all_to_all x1, waiting for transfers between devices, local(): lax.all_to_all(queries, 'head', split_axis=1, concat_axis=0, tiled=True)  14.8 us
    all_to_all x1, starting transfers between devices, local(): lax.all_to_all(keys, 'head', split_axis=1, concat_axis=0, tiled=True)  7.66 us
    all_to_all x1, starting transfers between devices, local(): lax.all_to_all(values, 'head', split_axis=1, concat_axis=0, tiled=True)  4.73 us
    all_to_all x1, starting transfers between devices, local(): lax.all_to_all(queries, 'head', split_axis=1, concat_axis=0, tiled=True)  4.59 us
  transfers between devices with their start and end apart: 5, of which 5 were waited for; matrix products, arithmetic and copies ran while one was open for 4% of the time, Pallas kernels for 0%

commit v1 on v0

--- a/solution.py
+++ b/solution.py
@@ -7,44 +7,35 @@
 
 
 def local(queries, keys, values, group_order, gain):
-    q_all, k_all, v_all = (
-        lax.all_to_all(queries, "head", split_axis=1, concat_axis=0, tiled=True),
-        lax.all_to_all(keys, "head", split_axis=1, concat_axis=0, tiled=True),
-        lax.all_to_all(values, "head", split_axis=1, concat_axis=0, tiled=True),
-    )
+    kv = jnp.stack([keys, values])
+    kv_all = lax.all_to_all(kv, "head", split_axis=2, concat_axis=1, tiled=True)
+    q_all = lax.all_to_all(queries, "head", split_axis=1, concat_axis=0, tiled=True)
     rows = q_all.shape[0]
     half = rows // 2
     local_heads = gain.shape[0] // DH
     pairs = lax.axis_size("seq")
     here = lax.axis_index("seq")
     qx = q_all.reshape(rows, local_heads, DH)
-    kx = k_all.reshape(rows, local_heads, DH)
-    vx = v_all.reshape(rows, local_heads, DH)
+    kx = kv_all[0].reshape(rows, local_heads, DH)
+    vx = kv_all[1].reshape(rows, local_heads, DH)
     kh = kx.reshape(2, half, local_heads, DH)
     vh = vx.reshape(2, half, local_heads, DH)
     state = jnp.einsum("jthd,jthe->jhde", kh, vh, preferred_element_type=jnp.float32).astype(
         jnp.bfloat16
     )
-    state = lax.optimization_barrier(state).astype(jnp.float32)
     order = group_order[0]
     low_first = order[0] < pairs
     lows = jnp.where(low_first, state[0], state[1])
     highs = jnp.where(low_first, state[1], state[0])
-    empty = jnp.zeros_like(lows)
-    low_sum = empty
-    high_sum = empty
-    piece_low = lax.all_gather(lows[None].astype(jnp.bfloat16), "seq", axis=0, tiled=True).astype(
-        jnp.float32
-    )
-    piece_high = lax.all_gather(highs[None].astype(jnp.bfloat16), "seq", axis=0, tiled=True).astype(
-        jnp.float32
-    )
-    owners = jnp.arange(piece_low.shape[0], dtype=jnp.int32)
+    both = (lows.astype(jnp.float32) + highs.astype(jnp.float32)).astype(jnp.bfloat16)
+    owners = jnp.arange(pairs, dtype=jnp.int32)
+    later = (owners > here)[:, None, None, None]
+    send = jnp.where(later, lows[None], both[None])
+    recv = lax.all_to_all(send, "seq", split_axis=0, concat_axis=0, tiled=True).astype(jnp.float32)
     below = (owners < here).astype(jnp.float32)[:, None, None, None]
-    other = (owners != here).astype(jnp.float32)[:, None, None, None]
     above = (owners > here).astype(jnp.float32)[:, None, None, None]
-    low_sum = low_sum + jnp.sum(piece_low * below, axis=0)
-    high_sum = high_sum + jnp.sum(piece_low * other + piece_high * above, axis=0)
+    low_sum = jnp.sum(recv * below, axis=0)
+    high_sum = low_sum + jnp.sum(recv * above, axis=0)
     first_pre = jnp.where(low_first, low_sum, high_sum).astype(jnp.bfloat16)
     second_pre = jnp.where(low_first, high_sum, low_sum).astype(jnp.bfloat16)
     index = jnp.arange(rows, dtype=jnp.int32)

time: 171 us -> 138 us (0.81)
  the two profiles are of different devices: /device:TPU:2 before, /device:TPU:1 now
where the time goes in v1:
time: 138 us; the launch traced here: 137 us
  waiting for transfers between devices  53.5 us (39%)
  local copies, waits for them, and re-layouts  47.6 us (34%)
  starting transfers between devices  25.1 us (18%)
  other arithmetic  5.54 us (4%)
  matrix products  4.3 us (3%)
    all_to_all x1, waiting for transfers between devices, local(): kv_all = lax.all_to_all(kv, 'head', split_axis=2, concat_axis=1, tiled=True)  31.1 us
    unnamed x10, local copies, waits for them, and re-layouts  23.8 us
    all_to_all x1, waiting for transfers between devices, local(): lax.all_to_all(send, 'seq', split_axis=0, concat_axis=0, tiled=True)  21.1 us
    all_to_all x1, starting transfers between devices, local(): kv_all = lax.all_to_all(kv, 'head', split_axis=2, concat_axis=1, tiled=True)  17.7 us
    all_to_all x1, local copies, waits for them, and re-layouts, local(): kv_all = lax.all_to_all(kv, 'head', split_axis=2, concat_axis=1, tiled=True)  9.02 us
    another operation x1, local copies, waits for them, and re-layouts, local(): kv = jnp.stack([keys, values])  6.84 us
    all_to_all x1, starting transfers between devices, local(): lax.all_to_all(queries, 'head', split_axis=1, concat_axis=0, tiled=True)  3.79 us
    all_to_all x1, starting transfers between devices, local(): lax.all_to_all(send, 'seq', split_axis=0, concat_axis=0, tiled=True)  3.56 us
  transfers between devices with their start and end apart: 3, of which 3 were waited for; matrix products, arithmetic and copies ran while one was open for 20% of the time, Pallas kernels for 0%

profile of v1, /device:TPU:1, one launch (start us, length us, event | category | flops | bytes accessed | tf_op | source)
XLA Modules:
  0.0 136.8 jit_solution(1540927092754109178)
XLA Ops:
  0.0 1.4 %pad_maximum_fusion = bf16[2,40,8192]{2,1,0:T(8,128)(2,1)S(1)} fusion(bf16[1,40,8192]{2,1,0:T(8,128)(2,1)} %bitcast.53, bf16[1,40,8192]{2,1,0:T(8,128)(2,1)} %bitcast.54), kind=kLoop, calls=%fused_computation.12 | loop fusion | flops 655360 | bytes 2621440 | tf_op jit(solution)/shard_map/stack | solution.py:10
  1.4 6.8 %copy.49 = bf16[2,40,8192]{1,0,2:T(2,128)(2,1)} copy(bf16[2,40,8192]{2,1,0:T(8,128)(2,1)S(1)} %pad_maximum_fusion) | data formatting | bytes 2621440 | tf_op jit(solution)/shard_map/stack | solution.py:10
  8.3 15.7 %reshape.166 = bf16[16,2,20480]{2,1,0:T(2,128)(2,1)} reshape(bf16[8192,2,40]{2,1,0:T(2,128)(2,1)} %bitcast.47) | data formatting | bytes 2621440
  24.0 17.7 %all-to-all-start = ((bf16[16,2,20480]{2,1,0:T(2,128)(2,1)}), bf16[16,2,20480]{2,1,0:T(2,128)(2,1)S(1)}, u32[]{:S(2)}, u32[]{:S(2)}) async-start(bf16[16,2,20480]{2,1,0:T(2,128)(2,1)} %reshape.166), calls=%async_computation | async-start | bytes 2621440 | tf_op jit(solution)/shard_map/all_to_all | solution.py:11
  41.8 0.9 copy.90
  42.6 0.6 fusion.42
  43.9 31.1 %all-to-all-done = bf16[16,2,20480]{2,1,0:T(2,128)(2,1)S(1)} async-done(((bf16[16,2,20480]{2,1,0:T(2,128)(2,1)}), bf16[16,2,20480]{2,1,0:T(2,128)(2,1)S(1)}, u32[]{:S(2)}, u32[]{:S(2)}) %all-to-all-start) | async-done | bytes 1310752 | tf_op jit(solution)/shard_map/all_to_all | solution.py:11
  75.0 3.8 %all-to-all-start.1 = ((bf16[40,16,512]{2,0,1:T(8,128)(2,1)}), bf16[40,16,512]{2,0,1:T(8,128)(2,1)S(1)}, u32[]{:S(2)}, u32[]{:S(2)}) async-start(bf16[40,16,512]{2,0,1:T(8,128)(2,1)} %bitcast.46), calls=%async_computation.1 | async-start | bytes 1310720 | tf_op jit(solution)/shard_map/all_to_all | solution.py:12
  78.8 7.6 %reshape.167 = bf16[8192,2,40]{2,1,0:T(2,128)(2,1)} reshape(bf16[16,2,20480]{2,1,0:T(2,128)(2,1)S(1)} %all-to-all-done) | data formatting | bytes 2621440
  86.4 9.0 %copy.50 = bf16[2,40,16,512]{3,1,2,0:T(8,128)(2,1)S(1)} copy(bf16[2,40,16,512]{1,0,3,2:T(2,128)(2,1)} %bitcast.48) | data formatting | bytes 2621440 | tf_op jit(solution)/shard_map/all_to_all | solution.py:11
  95.4 0.1 fusion.40
  95.5 0.2 reshape_reshape_squeeze.6
  95.7 0.2 reshape_reshape_squeeze.7
  95.9 0.4 convolution_convert_fusion
  96.4 1.1 broadcast_select_fusion
  97.5 1.3 all-to-all-done.1
  98.8 3.6 %all-to-all-start.2 = ((bf16[8,4,128,128]{3,2,1,0:T(8,128)(2,1)}), bf16[8,4,128,128]{3,2,1,0:T(8,128)(2,1)S(1)}, u32[]{:S(2)}, u32[]{:S(2)}) async-start(bf16[8,4,128,128]{3,2,1,0:T(8,128)(2,1)} %broadcast_select_fusion), calls=%async_computation.2 | async-start | bytes 2097152 | tf_op jit(solution)/shard_map/all_to_all | solution.py:34
  102.3 1.3 fusion.37
  103.6 1.1 broadcast_compare_fusion
  104.7 1.0 reshape.139
  105.7 0.8 fusion.41
  106.5 1.1 squeeze.7
  107.6 1.0 reshape_squeeze.6
  108.6 1.0 reshape_squeeze.7
  109.6 21.1 %all-to-all-done.2 = bf16[8,4,128,128]{3,2,1,0:T(8,128)(2,1)S(1)} async-done(((bf16[8,4,128,128]{3,2,1,0:T(8,128)(2,1)}), bf16[8,4,128,128]{3,2,1,0:T(8,128)(2,1)S(1)}, u32[]{:S(2)}, u32[]{:S(2)}) %all-to-all-start.2) | async-done | bytes 1048608 | tf_op jit(solution)/shard_map/all_to_all | solution.py:34
  130.8 0.4 fusion.8
  131.2 0.3 convolution_bitcast_fusion.1
  131.5 0.3 convolution_bitcast_fusion
  131.9 0.4 copy-done.1
  132.3 3.2 %multiply_reduce_fusion = (f32[640,4]{0,1:T(4,128)S(1)}, f32[640,4,128]{0,2,1:T(8,128)S(1)}) fusion(f32[320,4,128]{0,2,1:T(8,128)S(1)} %convolution_bitcast_fusion, f32[320,4,128]{0,2,1:T(8,128)S(1)} %convolution_bitcast_fusion.1, pred[640,640]{0,1:T(8,128)(4,1)} %broadcast_compare_fusion, bf16[640,4,128]{2,1,0:T(4,128)(2,1)S(1)} %copy-done.1, ...), kind=kOutput, calls=%fused_computation.14 | convolution fusion | flops 843445760 | bytes 5007360 | tf_op jit(solution)/shard_map/hts,she->the/dot_general | solution.py:46
  135.6 0.2 multiply_convert_fusion
  135.7 1.1 copy.62
  (14 shorter events, 0.2 us)
Async XLA Ops:
  24.0 17.8 %copy-start = (bf16[40,8192]{1,0:T(8,128)(2,1)S(1)}, bf16[40,8192]{1,0:T(8,128)(2,1)}, u32[]{:S(2)}) copy-start(bf16[40,8192]{1,0:T(8,128)(2,1)} %param.5) | copy-start | bytes 1966084
  24.0 51.0 %all-to-all-start = ((bf16[16,2,20480]{2,1,0:T(2,128)(2,1)}), bf16[16,2,20480]{2,1,0:T(2,128)(2,1)S(1)}, u32[]{:S(2)}, u32[]{:S(2)}) async-start(bf16[16,2,20480]{2,1,0:T(2,128)(2,1)} %reshape.166), calls=%async_computation | async-start | bytes 2621440 | tf_op jit(solution)/shard_map/all_to_all | solution.py:11
  41.7 0.9 copy-start.2
  75.0 23.7 %all-to-all-start.1 = ((bf16[40,16,512]{2,0,1:T(8,128)(2,1)}), bf16[40,16,512]{2,0,1:T(8,128)(2,1)S(1)}, u32[]{:S(2)}, u32[]{:S(2)}) async-start(bf16[40,16,512]{2,0,1:T(8,128)(2,1)} %bitcast.46), calls=%async_computation.1 | async-start | bytes 1310720 | tf_op jit(solution)/shard_map/all_to_all | solution.py:12
  98.8 32.0 %all-to-all-start.2 = ((bf16[8,4,128,128]{3,2,1,0:T(8,128)(2,1)}), bf16[8,4,128,128]{3,2,1,0:T(8,128)(2,1)S(1)}, u32[]{:S(2)}, u32[]{:S(2)}) async-start(bf16[8,4,128,128]{3,2,1,0:T(8,128)(2,1)} %broadcast_select_fusion), calls=%async_computation.2 | async-start | bytes 2097152 | tf_op jit(solution)/shard_map/all_to_all | solution.py:34
  131.2 1.1 copy-start.1
  132.3 3.3 %copy-start.3 = (f32[512]{0:T(512)S(1)}, f32[512]{0:T(512)}, u32[]{:S(2)}) copy-start(f32[512]{0:T(512)} %param.9) | copy-start | bytes 6148
